TPU v7x, 32 devices: a whole 2x2x4 slice. The times are simulated.
32 devices in a mesh: groups: 2 (over y), gz: 4 (over z), sec: 2 (over x), ch: 2 (over core).
Axes of the slice: x: 2, y: 2, z: 4, core: 2. Of those that a mesh axis runs over, the one named last changes fastest.
Arguments:
- coarse: bfloat16 [64, 32, 4, 256], P('ch', ('groups', 'gz', 'sec')), parts along dimension 1, may hold values from -6 to 6
- saved_pre: bfloat16 [32, 64, 8, 512], P('ch', ('groups', 'gz', 'sec')), parts along dimension 1, may hold values from -6 to 6
- out_grad: bfloat16 [32, 64, 8, 512], P('ch', ('groups', 'gz', 'sec')), parts along dimension 1, may hold values from -6 to 6
- up_weight: bfloat16 [27, 32, 64], replicated, may hold values from -0.21875 to 0.21875
- refine_weight: bfloat16 [27, 32, 32], replicated, may hold values from -0.21875 to 0.21875
Outputs:
- grad_coarse: bfloat16 [64, 32, 4, 256], P('ch', ('groups', 'gz', 'sec')), parts along dimension 1
- grad_up: float32 [54, 32, 64], P('groups', 'ch'), parts along dimension 0
- grad_refine: float32 [54, 32, 32], P('groups', None, 'ch'), parts along dimension 0
There are 2 independent parts, one for each index of `groups`. A program takes and returns all parts, laid end to end along the dimension named above; an argument that names none is the same for every part. Nothing has to cross between parts.
All inputs are finite; a program needn't handle non-finite values.
Results may differ from a plain program's by a relative error of at most 0.0049.
Values may be sent and summed in bfloat16 or wider, within the bound.
No kernel may reach another device: no remote copies, remote signals or barrier semaphores. Data moves between devices by JAX's collectives and lax.ppermute only.
A program may use at most 128 MiB of HBM per device.

v0:
```python
import jax
import jax.numpy as jnp
from jax import lax
from jax.sharding import PartitionSpec as P

leak_slope = 0.2


def padded(block, sides, width):
    for axis, dim in sides:
        count = lax.axis_size(axis)
        forward = [(i, i + 1) for i in range(count - 1)]
        forward.append((count - 1, 0))
        backward = [(target, source) for source, target in forward]
        low = lax.ppermute(
            lax.slice_in_dim(block, block.shape[dim] - width, None, axis=dim), axis, forward
        )
        high = lax.ppermute(lax.slice_in_dim(block, 0, width, axis=dim), axis, backward)
        block = jnp.concatenate([low, block, high], axis=dim)
    return block


def passed_along(block, axis, distance):
    devices = range(lax.axis_size(axis))
    route = [((i - distance) % len(devices), i) for i in devices]
    return lax.ppermute(block, axis, route)


def kernel_offsets():
    return [
        (along_z, along_x, along_y)
        for along_z in range(3)
        for along_x in range(3)
        for along_y in range(3)
    ]


def take_taps(source, along_z, along_x, along_y, coarse_z, coarse_x):
    selected = source[
        :, along_z : along_z + 2 * coarse_z : 2, along_x : along_x + 2 * coarse_x : 2, :
    ]
    return jnp.roll(selected, 1 - along_y, axis=3)[:, :, :, ::2]


def local(coarse, saved_pre, out_grad, up_weight, refine_weight):
    part_ch = saved_pre.shape[0]
    planes_z = saved_pre.shape[1]
    planes_x = saved_pre.shape[2]
    cells_y = saved_pre.shape[3]
    coarse_z = planes_z // 2
    coarse_x = planes_x // 2
    channel_start = lax.axis_index("ch") * part_ch
    pre_act = saved_pre.astype(jnp.float32)
    slopes = jnp.where(pre_act > 0, 1.0, leak_slope).astype(jnp.float32)
    hidden = (pre_act * slopes).astype(jnp.bfloat16)
    every_channel = lax.all_gather(out_grad, "ch", axis=0, tiled=True)
    rimmed_z = padded(every_channel, ((("gz", "sec"), 1),), 2)
    rimmed = jnp.pad(rimmed_z, ((0, 0), (0, 0), (2, 2), (0, 0)))
    refine_cols = lax.dynamic_slice_in_dim(refine_weight, channel_start, part_ch, 2)
    grad_hidden = jnp.zeros(pre_act.shape, jnp.float32)
    refine_terms = []
    for tap_number, (along_z, along_x, along_y) in enumerate(kernel_offsets()):
        shifted = rimmed[
            :,
            4 - 2 * along_z : 4 - 2 * along_z + planes_z,
            4 - 2 * along_x : 4 - 2 * along_x + planes_x,
            :,
        ]
        shifted = jnp.roll(shifted, 2 * (along_y - 1), axis=3)
        grad_hidden = grad_hidden + jnp.einsum(
            "oc,ozxy->czxy", refine_cols[tap_number], shifted, preferred_element_type=jnp.float32
        )
        refine_terms.append(
            jnp.einsum("ozxy,czxy->oc", shifted, hidden, preferred_element_type=jnp.float32)
        )
    grad_pre = (grad_hidden * slopes).astype(jnp.bfloat16)
    below_z = passed_along(grad_pre[:, planes_z - 1 :, :, :], ("gz", "sec"), 1)
    raised_z = jnp.concatenate([below_z, grad_pre], axis=1)
    extended = jnp.pad(raised_z, ((0, 0), (0, 0), (1, 0), (0, 0)))
    selections = [
        take_taps(extended, along_z, along_x, along_y, coarse_z, coarse_x)
        for along_z, along_x, along_y in kernel_offsets()
    ]
    all_coarse = lax.all_gather(coarse, "ch", axis=0, tiled=True)
    up_terms = [
        jnp.einsum("czxy,fzxy->fc", all_coarse, selected, preferred_element_type=jnp.float32)
        for selected in selections
    ]
    up_rows = lax.dynamic_slice_in_dim(up_weight, channel_start, part_ch, 1)
    running = jnp.zeros((coarse.shape[0] * lax.axis_size("ch"),) + coarse.shape[1:], jnp.float32)
    for tap_number, selected in enumerate(selections):
        weight_block = up_rows[tap_number]
        running = running + jnp.einsum(
            "fc,fzxy->czxy", weight_block, selected, preferred_element_type=jnp.float32
        )
    coarse_summed = lax.psum_scatter(running, "ch", scatter_dimension=0, tiled=True)
    grad_coarse = coarse_summed.astype(jnp.bfloat16)
    up_summed, refine_summed = lax.psum(
        (jnp.stack(up_terms), jnp.stack(refine_terms)), ("gz", "sec")
    )
    fine_total = planes_z * lax.axis_size("gz") * lax.axis_size("sec") * planes_x * cells_y
    coarse_total = fine_total // 8
    grad_up = up_summed * float(coarse_total) ** (-0.5)
    grad_refine = refine_summed * float(fine_total) ** (-0.5)
    return (grad_coarse, grad_up, grad_refine)


def solution(mesh):
    placed = (
        P("ch", ("groups", "gz", "sec"), None, None),
        P("ch", ("groups", "gz", "sec"), None, None),
        P("ch", ("groups", "gz", "sec"), None, None),
        P(),
        P(),
    )
    return jax.shard_map(
        local,
        mesh=mesh,
        in_specs=placed,
        out_specs=(
            P("ch", ("groups", "gz", "sec"), None, None),
            P("groups", "ch", None),
            P("groups", None, "ch"),
        ),
        check_vma=False,
    )
```

profile of v0, /device:TPU:0, one launch (start us, length us, event | category | flops | bytes accessed | tf_op | source)
XLA Modules:
  0.0 347.9 jit_solution(7144376566447000384)
XLA Ops:
  12.5 8.8 %all-gather.2.cloned.1.call-done = bf16[32,4,8,512]{3,0,2,1:T(8,128)(2,1)} async-done(((bf16[16,4,8,512]{3,0,2,1:T(8,128)(2,1)}), bf16[32,4,8,512]{3,0,2,1:T(8,128)(2,1)}) %all-gather.2.cloned.1.call-update) | async-done | bytes 1048592 | tf_op jit(solution)/shard_map/all_gather | solution.py:56
  24.5 3.0 collective-permute-start.1
  29.0 18.3 %collective-permute-done = bf16[32,2,8,512]{3,0,2,1:T(8,128)(2,1)S(1)} collective-permute-done((bf16[32,2,8,512]{3,0,2,1:T(8,128)(2,1)S(1)}, bf16[32,2,8,512]{3,0,2,1:T(8,128)(2,1)S(1)}, u32[]{:S(2)}, u32[]{:S(2)}) %collective-permute-start) | collective-permute-done | bytes 524320 | tf_op jit(solution)/shard_map/ppermute | solution.py:15
  50.0 4.9 %fusion.280 = (bf16[32,4,8,510]{3,0,2,1:T(8,128)(2,1)S(1)}, bf16[32,4,8,510]{3,0,2,1:T(8,128)(2,1)S(1)}, bf16[32,4,8,510]{3,0,2,1:T(8,128)(2,1)S(1)}, bf16[32,4,...) fusion(bf16[32,8,12,512]{3,0,2,1:T(8,128)(2,1)S(1)} %fusion.5), kind=kLoop, calls=%fused_computation.425 | loop fusion | bytes 25067520 | tf_op jit(solution)/shard_map/jit(_roll_static)/slice | solution.py:69
  100.4 6.5 %collective-permute-done.2 = bf16[16,1,8,512]{3,0,2,1:T(8,128)(2,1)S(1)} collective-permute-done((bf16[16,1,8,512]{3,0,2,1:T(8,128)(2,1)S(1)}, bf16[16,1,8,512]{3,0,2,1:T(8,128)(2,1)S(1)}, u32[]{:S(2)}, u32[]{:S(2)}) %collective-permute-start.2) | collective-permute-done | bytes 131104 | tf_op jit(solution)/shard_map/ppermute | solution.py:26
  109.2 4.1 %slice.685 = bf16[16,2,4,256]{3,0,2,1:T(8,128)(2,1)} slice(bf16[16,2,4,512]{3,0,2,1:T(8,128)(2,1)} %copy-done.2), slice={[0:16:1], [0:2:1], [0:4:1], [0:512:2]} | slice | bytes 131072 | tf_op jit(solution)/shard_map/slice | solution.py:42
  116.6 3.8 %slice.696 = bf16[16,2,4,256]{3,0,2,1:T(8,128)(2,1)} slice(bf16[16,2,4,512]{3,0,2,1:T(8,128)(2,1)} %get-tuple-element.59), slice={[0:16:1], [0:2:1], [0:4:1], [0:512:2]} | slice | bytes 131072 | tf_op jit(solution)/shard_map/slice | solution.py:42
  159.2 3.3 slice.700
  164.2 3.8 %slice.705 = bf16[16,2,4,256]{3,0,2,1:T(8,128)(2,1)} slice(bf16[16,2,4,512]{3,0,2,1:T(8,128)(2,1)} %pad_maximum_fusion.22), slice={[0:16:1], [0:2:1], [0:4:1], [0:512:2]} | slice | bytes 131072 | tf_op jit(solution)/shard_map/slice | solution.py:42
  169.6 3.2 slice.711
  174.5 3.8 %slice.716 = bf16[16,2,4,256]{3,0,2,1:T(8,128)(2,1)} slice(bf16[16,2,4,512]{3,0,2,1:T(8,128)(2,1)} %pad_maximum_fusion.24), slice={[0:16:1], [0:2:1], [0:4:1], [0:512:2]} | slice | bytes 131072 | tf_op jit(solution)/shard_map/slice | solution.py:42
  179.9 3.2 slice.722
  184.7 3.8 %slice.727 = bf16[16,2,4,256]{3,0,2,1:T(8,128)(2,1)} slice(bf16[16,2,4,512]{3,0,2,1:T(8,128)(2,1)} %pad_maximum_fusion.26), slice={[0:16:1], [0:2:1], [0:4:1], [0:512:2]} | slice | bytes 131072 | tf_op jit(solution)/shard_map/slice | solution.py:42
  190.2 3.8 %slice.733 = bf16[16,2,4,256]{3,0,2,1:T(8,128)(2,1)} slice(bf16[16,2,4,512]{3,0,2,1:T(8,128)(2,1)} %pad_maximum_fusion.27), slice={[0:16:1], [0:2:1], [0:4:1], [0:512:2]} | slice | bytes 131072 | tf_op jit(solution)/shard_map/slice | solution.py:42
  195.6 3.8 %slice.738 = bf16[16,2,4,256]{3,0,2,1:T(8,128)(2,1)} slice(bf16[16,2,4,512]{3,0,2,1:T(8,128)(2,1)} %pad_maximum_fusion.28), slice={[0:16:1], [0:2:1], [0:4:1], [0:512:2]} | slice | bytes 131072 | tf_op jit(solution)/shard_map/slice | solution.py:42
  201.0 3.8 %slice.744 = bf16[16,2,4,256]{3,0,2,1:T(8,128)(2,1)} slice(bf16[16,2,4,512]{3,0,2,1:T(8,128)(2,1)} %pad_maximum_fusion.29), slice={[0:16:1], [0:2:1], [0:4:1], [0:512:2]} | slice | bytes 131072 | tf_op jit(solution)/shard_map/slice | solution.py:42
  206.4 3.8 %slice.749 = bf16[16,2,4,256]{3,0,2,1:T(8,128)(2,1)} slice(bf16[16,2,4,512]{3,0,2,1:T(8,128)(2,1)} %pad_maximum_fusion.30), slice={[0:16:1], [0:2:1], [0:4:1], [0:512:2]} | slice | bytes 131072 | tf_op jit(solution)/shard_map/slice | solution.py:42
  211.8 3.8 %slice.755 = bf16[16,2,4,256]{3,0,2,1:T(8,128)(2,1)} slice(bf16[16,2,4,512]{3,0,2,1:T(8,128)(2,1)} %pad_maximum_fusion.31), slice={[0:16:1], [0:2:1], [0:4:1], [0:512:2]} | slice | bytes 131072 | tf_op jit(solution)/shard_map/slice | solution.py:42
  217.3 3.8 %slice.760 = bf16[16,2,4,256]{3,0,2,1:T(8,128)(2,1)} slice(bf16[16,2,4,512]{3,0,2,1:T(8,128)(2,1)} %pad_maximum_fusion.32), slice={[0:16:1], [0:2:1], [0:4:1], [0:512:2]} | slice | bytes 131072 | tf_op jit(solution)/shard_map/slice | solution.py:42
  222.7 3.9 %slice.766 = bf16[16,2,4,256]{3,0,2,1:T(8,128)(2,1)} slice(bf16[16,2,4,512]{3,0,2,1:T(8,128)(2,1)} %pad_maximum_fusion.33), slice={[0:16:1], [0:2:1], [0:4:1], [0:512:2]} | slice | bytes 131072 | tf_op jit(solution)/shard_map/slice | solution.py:42
  228.3 3.8 %slice.771 = bf16[16,2,4,256]{3,0,2,1:T(8,128)(2,1)} slice(bf16[16,2,4,512]{3,0,2,1:T(8,128)(2,1)} %pad_maximum_fusion.34), slice={[0:16:1], [0:2:1], [0:4:1], [0:512:2]} | slice | bytes 131072 | tf_op jit(solution)/shard_map/slice | solution.py:42
  233.7 3.2 slice.777
  292.9 36.5 %psum.15 = f32[27,32,16]{1,2,0:T(8,128)S(1)} all-reduce(f32[27,32,16]{1,2,0:T(8,128)S(1)} %fusion.16), channel_id=1, replica_groups=mesh['groups'=2,'gz'=4,'sec'=2,'ch'=2] {'gz','sec'}, use_global_device_ids=true, to_apply=%region_2.3 | all-reduce | flops 13824 | bytes 110592 | tf_op jit(solution)/shard_map/psum | solution.py:98
  331.8 7.7 %reduce-scatter.2.cloned.1.call-done = f32[32,2,4,256]{3,0,2,1:T(8,128)} async-done(((f32[64,2,4,256]{3,0,2,1:T(8,128)}), f32[32,2,4,256]{3,0,2,1:T(8,128)}) %reduce-scatter.2.cloned.1.call-update) | async-done | bytes 262160 | tf_op jit(solution)/shard_map/reduce_scatter | solution.py:96
  (279 shorter events, 184.9 us)
Async XLA Ops:
  7.2 79.5 %copy-start = (bf16[27,32,32]{2,1,0:T(8,128)(2,1)S(1)}, bf16[27,32,32]{2,1,0:T(8,128)(2,1)}, u32[]{:S(2)}) copy-start(bf16[27,32,32]{2,1,0:T(8,128)(2,1)} %param.9) | copy-start | bytes 165892
  7.2 14.1 %all-gather.2.cloned.1.call-start = ((), (), s32[]{:S(2)}) async-start(), calls=%async_computation.1 | async-start | bytes 1572864 | tf_op jit(solution)/shard_map/all_gather | solution.py:56
  9.4 320.7 %all-reduce.4.cloned.1.call-start = ((), (), s32[]{:S(2)}) async-start(), calls=%async_computation.3 | async-start | bytes 442368 | tf_op jit(solution)/shard_map/psum | solution.py:98
  22.7 24.7 %collective-permute-start = (bf16[32,2,8,512]{3,0,2,1:T(8,128)(2,1)S(1)}, bf16[32,2,8,512]{3,0,2,1:T(8,128)(2,1)S(1)}, u32[]{:S(2)}, u32[]{:S(2)}) collective-permute-start(bf16[32,2,8,512]{3,0,2,1:T(8,128)(2,1)S(1)} %get-tuple-element.50), channel_id=1, source_target_pairs={{0,2},{2,4},{4,6},{6,8},{8,10},{10,12},{12,14},{14,0},{1,3},{3,5},... | collective-permute-start | bytes 1572872 | tf_op jit(solution)/shard_map/ppermute | solution.py:15
  24.5 25.1 %collective-permute-start.1 = (bf16[32,2,8,512]{3,0,2,1:T(8,128)(2,1)S(1)}, bf16[32,2,8,512]{3,0,2,1:T(8,128)(2,1)S(1)}, u32[]{:S(2)}, u32[]{:S(2)}) collective-permute-start(bf16[32,2,8,512]{3,0,2,1:T(8,128)(2,1)S(1)} %get-tuple-element.51), channel_id=1, source_target_pairs={{2,0},{4,2},{6,4},{8,6},{10,8},{12,10},{14,12},{0,14},{3,1},{5,3},... | collective-permute-start | bytes 1572872 | tf_op jit(solution)/shard_map/ppermute | solution.py:18
  99.2 7.7 %collective-permute-start.2 = (bf16[16,1,8,512]{3,0,2,1:T(8,128)(2,1)S(1)}, bf16[16,1,8,512]{3,0,2,1:T(8,128)(2,1)S(1)}, u32[]{:S(2)}, u32[]{:S(2)}) collective-permute-start(bf16[16,1,8,512]{3,0,2,1:T(8,128)(2,1)S(1)} %slice.824), channel_id=1, source_target_pairs={{14,0},{0,2},{2,4},{4,6},{6,8},{8,10},{10,12},{12,14},{15,1},{1,3}... | collective-permute-start | bytes 393224 | tf_op jit(solution)/shard_map/ppermute | solution.py:26
  127.9 22.3 %copy-start.41 = (bf16[16,2,4,1]{3,0,2,1:T(8,128)(2,1)S(1)}, bf16[16,2,4,1]{3,0,2,1:T(8,128)(2,1)}, u32[]{:S(2)}) copy-start(bf16[16,2,4,1]{3,0,2,1:T(8,128)(2,1)} %get-tuple-element.95) | copy-start | bytes 772
  136.3 31.7 %copy-start.40 = (bf16[16,2,4,1]{3,0,2,1:T(8,128)(2,1)S(1)}, bf16[16,2,4,1]{3,0,2,1:T(8,128)(2,1)}, u32[]{:S(2)}) copy-start(bf16[16,2,4,1]{3,0,2,1:T(8,128)(2,1)} %get-tuple-element.87) | copy-start | bytes 772
  143.1 40.0 %copy-start.39 = (bf16[16,2,4,1]{3,0,2,1:T(8,128)(2,1)S(1)}, bf16[16,2,4,1]{3,0,2,1:T(8,128)(2,1)}, u32[]{:S(2)}) copy-start(bf16[16,2,4,1]{3,0,2,1:T(8,128)(2,1)} %get-tuple-element.80) | copy-start | bytes 772
  143.8 44.7 %copy-start.37 = (bf16[16,2,4,1]{3,0,2,1:T(8,128)(2,1)S(1)}, bf16[16,2,4,1]{3,0,2,1:T(8,128)(2,1)}, u32[]{:S(2)}) copy-start(bf16[16,2,4,1]{3,0,2,1:T(8,128)(2,1)} %get-tuple-element.79) | copy-start | bytes 772
  146.3 47.7 %copy-start.38 = (bf16[16,2,4,1]{3,0,2,1:T(8,128)(2,1)S(1)}, bf16[16,2,4,1]{3,0,2,1:T(8,128)(2,1)}, u32[]{:S(2)}) copy-start(bf16[16,2,4,1]{3,0,2,1:T(8,128)(2,1)} %get-tuple-element.76) | copy-start | bytes 772
  150.2 49.1 %copy-start.36 = (bf16[16,2,4,1]{3,0,2,1:T(8,128)(2,1)S(1)}, bf16[16,2,4,1]{3,0,2,1:T(8,128)(2,1)}, u32[]{:S(2)}) copy-start(bf16[16,2,4,1]{3,0,2,1:T(8,128)(2,1)} %get-tuple-element.75) | copy-start | bytes 772
  157.6 52.6 %copy-start.35 = (bf16[16,2,4,1]{3,0,2,1:T(8,128)(2,1)S(1)}, bf16[16,2,4,1]{3,0,2,1:T(8,128)(2,1)}, u32[]{:S(2)}) copy-start(bf16[16,2,4,1]{3,0,2,1:T(8,128)(2,1)} %get-tuple-element.71) | copy-start | bytes 772
  188.5 50.1 %copy-start.8 = (bf16[16,2,4,256]{3,0,2,1:T(8,128)(2,1)S(1)}, bf16[16,2,4,256]{3,0,2,1:T(8,128)(2,1)}, u32[]{:S(2)}) copy-start(bf16[16,2,4,256]{3,0,2,1:T(8,128)(2,1)} %slice.685) | copy-start | bytes 196612
  201.0 40.8 %copy-start.7 = (bf16[16,2,4,256]{3,0,2,1:T(8,128)(2,1)S(1)}, bf16[16,2,4,256]{3,0,2,1:T(8,128)(2,1)}, u32[]{:S(2)}) copy-start(bf16[16,2,4,256]{3,0,2,1:T(8,128)(2,1)} %slice.696) | copy-start | bytes 196612
  211.8 33.2 %copy-start.6 = (bf16[16,2,4,256]{3,0,2,1:T(8,128)(2,1)S(1)}, bf16[16,2,4,256]{3,0,2,1:T(8,128)(2,1)}, u32[]{:S(2)}) copy-start(bf16[16,2,4,256]{3,0,2,1:T(8,128)(2,1)} %slice.707) | copy-start | bytes 196612
  236.9 9.7 %copy-start.18 = (bf16[16,2,4,256]{3,0,2,1:T(8,128)(2,1)S(1)}, bf16[16,2,4,256]{3,0,2,1:T(8,128)(2,1)}, u32[]{:S(2)}) copy-start(bf16[16,2,4,256]{3,0,2,1:T(8,128)(2,1)} %slice.716) | copy-start | bytes 196612
  236.9 12.1 %copy-start.20 = (bf16[16,2,4,256]{3,0,2,1:T(8,128)(2,1)S(1)}, bf16[16,2,4,256]{3,0,2,1:T(8,128)(2,1)}, u32[]{:S(2)}) copy-start(bf16[16,2,4,256]{3,0,2,1:T(8,128)(2,1)} %slice.727) | copy-start | bytes 196612
  239.3 11.2 %copy-start.9 = (bf16[16,2,4,256]{3,0,2,1:T(8,128)(2,1)S(1)}, bf16[16,2,4,256]{3,0,2,1:T(8,128)(2,1)}, u32[]{:S(2)}) copy-start(bf16[16,2,4,256]{3,0,2,1:T(8,128)(2,1)} %slice.733) | copy-start | bytes 196612
  240.1 11.2 %copy-start.22 = (bf16[16,2,4,256]{3,0,2,1:T(8,128)(2,1)S(1)}, bf16[16,2,4,256]{3,0,2,1:T(8,128)(2,1)}, u32[]{:S(2)}) copy-start(bf16[16,2,4,256]{3,0,2,1:T(8,128)(2,1)} %slice.738) | copy-start | bytes 196612
  242.6 10.3 %copy-start.11 = (bf16[16,2,4,256]{3,0,2,1:T(8,128)(2,1)S(1)}, bf16[16,2,4,256]{3,0,2,1:T(8,128)(2,1)}, u32[]{:S(2)}) copy-start(bf16[16,2,4,256]{3,0,2,1:T(8,128)(2,1)} %slice.744) | copy-start | bytes 196612
  243.4 10.3 %copy-start.24 = (bf16[16,2,4,256]{3,0,2,1:T(8,128)(2,1)S(1)}, bf16[16,2,4,256]{3,0,2,1:T(8,128)(2,1)}, u32[]{:S(2)}) copy-start(bf16[16,2,4,256]{3,0,2,1:T(8,128)(2,1)} %slice.749) | copy-start | bytes 196612
  248.9 9.4 %copy-start.28 = (bf16[16,2,4,256]{3,0,2,1:T(8,128)(2,1)S(1)}, bf16[16,2,4,256]{3,0,2,1:T(8,128)(2,1)}, u32[]{:S(2)}) copy-start(bf16[16,2,4,256]{3,0,2,1:T(8,128)(2,1)} %slice.771) | copy-start | bytes 196612
  260.8 78.7 %reduce-scatter.2.cloned.1.call-start = ((), (), s32[]{:S(2)}) async-start(), calls=%async_computation.2 | async-start | bytes 786432 | tf_op jit(solution)/shard_map/reduce_scatter | solution.py:96
  (24 other events, 97.3 us)
Sparse Core Ops, SparseCore 0:
  9.6 11.7 all-gather.1
  260.9 68.8 all-reduce.3
  332.2 7.2 reduce-scatter.1
where the time goes:
time: 354 us; the launch traced here: 348 us
  local copies, waits for them, and re-layouts  120 us (34%)
  matrix products  87.3 us (25%)
  waiting for transfers between devices  43.6 us (12%)
  blocking collectives  38.6 us (11%)
  other arithmetic  38.6 us (11%)
  between operations  14.9 us (4%)
  starting transfers between devices  5.22 us (1%)
    slice x45, local copies, waits for them, and re-layouts, take_taps(): return jnp.roll(selected, 1 - along_y, axis=3)[:, :, :, ::2]  101 us
    psum x1, blocking collectives, local(): lax.psum((jnp.stack(up_terms), jnp.stack(refine_terms)), ('gz', 'sec'))  36.5 us
    concatenate x18, other arithmetic, take_taps(): return jnp.roll(selected, 1 - along_y, axis=3)[:, :, :, ::2]  27.9 us
    dot_general x27, matrix products, local(): jnp.einsum('fc,fzxy->czxy', weight_block, selected, preferred_element_typ...  26.9 us
    dot_general x27, matrix products, local(): jnp.einsum('ozxy,czxy->oc', shifted, hidden, preferred_element_type=jnp.f...  25 us
    dot_general x27, matrix products, local(): jnp.einsum('czxy,fzxy->fc', all_coarse, selected, preferred_element_type=...  23.8 us
    ppermute x1, waiting for transfers between devices, padded(): lax.ppermute(lax.slice_in_dim(block, block.shape[dim] - width, None, axis...  18.3 us
    dot_general x27, matrix products, local(): jnp.einsum('oc,ozxy->czxy', refine_cols[tap_number], shifted, preferred_e...  11.6 us
  transfers between devices with their start and end apart: 6, of which 5 were waited for; matrix products, arithmetic and copies ran while one was open for 11% of the time, Pallas kernels for 0%

commit v1 on v0

--- a/solution.py
+++ b/solution.py
@@ -96,7 +96,7 @@
     coarse_summed = lax.psum_scatter(running, "ch", scatter_dimension=0, tiled=True)
     grad_coarse = coarse_summed.astype(jnp.bfloat16)
     up_summed, refine_summed = lax.psum(
-        (jnp.stack(up_terms), jnp.stack(refine_terms)), ("gz", "sec")
+        lax.psum((jnp.stack(up_terms), jnp.stack(refine_terms)), "sec"), "gz"
     )
     fine_total = planes_z * lax.axis_size("gz") * lax.axis_size("sec") * planes_x * cells_y
     coarse_total = fine_total // 8

time: 354 us -> 308 us (0.87)
  matrix products: 87.3 us -> 67 us
  local copies, waits for them, and re-layouts: 120 us -> 106 us
  blocking collectives: 38.6 us -> 33.5 us
  other arithmetic: 38.6 us -> 34.4 us
    dot_general x27, matrix products: 23.8 us -> 4.99 us  [local(): jnp.einsum('czxy,fzxy->fc', all_coarse, selected, preferred_element_type=...]
    slice x45, local copies, waits for them, and re-layouts: 101 us -> 86.3 us  [take_taps(): return jnp.roll(selected, 1 - along_y, axis=3)[:, :, :, ::2]]
    psum x1 -> x2, blocking collectives: 36.5 us -> 31.4 us  [the longest x1 22 us: local(): lax.psum(lax.psum((jnp.stack(up_terms), jnp.stack(refine_terms)), 'sec'),...]
    concatenate x18, other arithmetic: 27.9 us -> 23.6 us  [take_taps(): return jnp.roll(selected, 1 - along_y, axis=3)[:, :, :, ::2]]
  transfers between devices with their start and end apart: 6 -> 7, of which waited for: 5 -> 5; matrix products, arithmetic and copies ran while one was open for 11% -> 11% of each run, Pallas kernels for 0% -> 0%
where the time goes in v1:
time: 308 us; the launch traced here: 302 us
  local copies, waits for them, and re-layouts  106 us (34%)
  matrix products  67 us (22%)
  waiting for transfers between devices  41.5 us (13%)
  other arithmetic  34.4 us (11%)
  blocking collectives  33.5 us (11%)
  between operations  14.9 us (5%)
  starting transfers between devices  5.28 us (2%)
    slice x45, local copies, waits for them, and re-layouts, take_taps(): return jnp.roll(selected, 1 - along_y, axis=3)[:, :, :, ::2]  86.3 us
    dot_general x27, matrix products, local(): jnp.einsum('fc,fzxy->czxy', weight_block, selected, preferred_element_typ...  26.3 us
    dot_general x27, matrix products, local(): jnp.einsum('ozxy,czxy->oc', shifted, hidden, preferred_element_type=jnp.f...  24.1 us
    concatenate x18, other arithmetic, take_taps(): return jnp.roll(selected, 1 - along_y, axis=3)[:, :, :, ::2]  23.6 us
    psum x1, blocking collectives, local(): lax.psum(lax.psum((jnp.stack(up_terms), jnp.stack(refine_terms)), 'sec'),...  22 us
    ppermute x1, waiting for transfers between devices, padded(): lax.ppermute(lax.slice_in_dim(block, block.shape[dim] - width, None, axis...  18.3 us
    dot_general x27, matrix products, local(): jnp.einsum('oc,ozxy->czxy', refine_cols[tap_number], shifted, preferred_e...  11.6 us
    slice x8, local copies, waits for them, and re-layouts, local(): shifted = jnp.roll(shifted, 2 * (along_y - 1), axis=3)  10.1 us
  transfers between devices with their start and end apart: 7, of which 5 were waited for; matrix products, arithmetic and copies ran while one was open for 11% of the time, Pallas kernels for 0%

profile of v1, /device:TPU:0, one launch (start us, length us, event | category | flops | bytes accessed | tf_op | source)
XLA Modules:
  0.0 302.3 jit_solution(13494542343058815466)
XLA Ops:
  12.5 8.8 %all-gather.2.cloned.1.call-done = bf16[32,4,8,512]{3,0,2,1:T(8,128)(2,1)} async-done(((bf16[16,4,8,512]{3,0,2,1:T(8,128)(2,1)}), bf16[32,4,8,512]{3,0,2,1:T(8,128)(2,1)}) %all-gather.2.cloned.1.call-update) | async-done | bytes 1048592 | tf_op jit(solution)/shard_map/all_gather | solution.py:56
  24.5 3.0 collective-permute-start.1
  29.0 18.3 %collective-permute-done = bf16[32,2,8,512]{3,0,2,1:T(8,128)(2,1)S(1)} collective-permute-done((bf16[32,2,8,512]{3,0,2,1:T(8,128)(2,1)S(1)}, bf16[32,2,8,512]{3,0,2,1:T(8,128)(2,1)S(1)}, u32[]{:S(2)}, u32[]{:S(2)}) %collective-permute-start) | collective-permute-done | bytes 524320 | tf_op jit(solution)/shard_map/ppermute | solution.py:15
  50.0 4.9 %fusion.280 = (bf16[32,4,8,510]{3,0,2,1:T(8,128)(2,1)S(1)}, bf16[32,4,8,510]{3,0,2,1:T(8,128)(2,1)S(1)}, bf16[32,4,8,510]{3,0,2,1:T(8,128)(2,1)S(1)}, bf16[32,4,...) fusion(bf16[32,8,12,512]{3,0,2,1:T(8,128)(2,1)S(1)} %fusion.5), kind=kLoop, calls=%fused_computation.425 | loop fusion | bytes 25067520 | tf_op jit(solution)/shard_map/jit(_roll_static)/slice | solution.py:69
  102.5 6.5 %collective-permute-done.2 = bf16[16,1,8,512]{3,0,2,1:T(8,128)(2,1)S(1)} collective-permute-done((bf16[16,1,8,512]{3,0,2,1:T(8,128)(2,1)S(1)}, bf16[16,1,8,512]{3,0,2,1:T(8,128)(2,1)S(1)}, u32[]{:S(2)}, u32[]{:S(2)}) %collective-permute-start.2) | collective-permute-done | bytes 131104 | tf_op jit(solution)/shard_map/ppermute | solution.py:26
  110.6 2.7 slice.685
  152.7 2.5 slice.700
  156.9 3.2 %slice.705 = bf16[16,2,4,256]{3,0,2,1:T(8,128)(2,1)S(1)} slice(bf16[16,2,4,512]{3,0,2,1:T(8,128)(2,1)} %pad_maximum_fusion.22), slice={[0:16:1], [0:2:1], [0:4:1], [0:512:2]} | slice | bytes 131072 | tf_op jit(solution)/shard_map/slice | solution.py:42
  161.8 3.2 %slice.711 = bf16[16,2,4,256]{3,0,2,1:T(8,128)(2,1)S(1)} slice(bf16[16,2,4,512]{3,0,2,1:T(8,128)(2,1)} %pad_maximum_fusion.23), slice={[0:16:1], [0:2:1], [0:4:1], [0:512:2]} | slice | bytes 131072 | tf_op jit(solution)/shard_map/slice | solution.py:42
  166.6 3.2 %slice.716 = bf16[16,2,4,256]{3,0,2,1:T(8,128)(2,1)S(1)} slice(bf16[16,2,4,512]{3,0,2,1:T(8,128)(2,1)} %pad_maximum_fusion.24), slice={[0:16:1], [0:2:1], [0:4:1], [0:512:2]} | slice | bytes 131072 | tf_op jit(solution)/shard_map/slice | solution.py:42
  170.5 3.2 %slice.722 = bf16[16,2,4,256]{3,0,2,1:T(8,128)(2,1)S(1)} slice(bf16[16,2,4,512]{3,0,2,1:T(8,128)(2,1)} %pad_maximum_fusion.25), slice={[0:16:1], [0:2:1], [0:4:1], [0:512:2]} | slice | bytes 131072 | tf_op jit(solution)/shard_map/slice | solution.py:42
  175.4 3.2 %slice.727 = bf16[16,2,4,256]{3,0,2,1:T(8,128)(2,1)S(1)} slice(bf16[16,2,4,512]{3,0,2,1:T(8,128)(2,1)} %pad_maximum_fusion.26), slice={[0:16:1], [0:2:1], [0:4:1], [0:512:2]} | slice | bytes 131072 | tf_op jit(solution)/shard_map/slice | solution.py:42
  180.2 3.2 %slice.733 = bf16[16,2,4,256]{3,0,2,1:T(8,128)(2,1)S(1)} slice(bf16[16,2,4,512]{3,0,2,1:T(8,128)(2,1)} %pad_maximum_fusion.27), slice={[0:16:1], [0:2:1], [0:4:1], [0:512:2]} | slice | bytes 131072 | tf_op jit(solution)/shard_map/slice | solution.py:42
  185.0 3.2 %slice.738 = bf16[16,2,4,256]{3,0,2,1:T(8,128)(2,1)S(1)} slice(bf16[16,2,4,512]{3,0,2,1:T(8,128)(2,1)} %pad_maximum_fusion.28), slice={[0:16:1], [0:2:1], [0:4:1], [0:512:2]} | slice | bytes 131072 | tf_op jit(solution)/shard_map/slice | solution.py:42
  188.9 3.2 %slice.744 = bf16[16,2,4,256]{3,0,2,1:T(8,128)(2,1)S(1)} slice(bf16[16,2,4,512]{3,0,2,1:T(8,128)(2,1)} %pad_maximum_fusion.29), slice={[0:16:1], [0:2:1], [0:4:1], [0:512:2]} | slice | bytes 131072 | tf_op jit(solution)/shard_map/slice | solution.py:42
  193.8 3.2 %slice.749 = bf16[16,2,4,256]{3,0,2,1:T(8,128)(2,1)S(1)} slice(bf16[16,2,4,512]{3,0,2,1:T(8,128)(2,1)} %pad_maximum_fusion.30), slice={[0:16:1], [0:2:1], [0:4:1], [0:512:2]} | slice | bytes 131072 | tf_op jit(solution)/shard_map/slice | solution.py:42
  198.6 3.2 %slice.755 = bf16[16,2,4,256]{3,0,2,1:T(8,128)(2,1)S(1)} slice(bf16[16,2,4,512]{3,0,2,1:T(8,128)(2,1)} %pad_maximum_fusion.31), slice={[0:16:1], [0:2:1], [0:4:1], [0:512:2]} | slice | bytes 131072 | tf_op jit(solution)/shard_map/slice | solution.py:42
  203.4 3.2 %slice.760 = bf16[16,2,4,256]{3,0,2,1:T(8,128)(2,1)S(1)} slice(bf16[16,2,4,512]{3,0,2,1:T(8,128)(2,1)} %pad_maximum_fusion.32), slice={[0:16:1], [0:2:1], [0:4:1], [0:512:2]} | slice | bytes 131072 | tf_op jit(solution)/shard_map/slice | solution.py:42
  207.4 3.4 %slice.766 = bf16[16,2,4,256]{3,0,2,1:T(8,128)(2,1)S(1)} slice(bf16[16,2,4,512]{3,0,2,1:T(8,128)(2,1)} %pad_maximum_fusion.33), slice={[0:16:1], [0:2:1], [0:4:1], [0:512:2]} | slice | bytes 131072 | tf_op jit(solution)/shard_map/slice | solution.py:42
  212.4 3.2 %slice.771 = bf16[16,2,4,256]{3,0,2,1:T(8,128)(2,1)S(1)} slice(bf16[16,2,4,512]{3,0,2,1:T(8,128)(2,1)} %pad_maximum_fusion.34), slice={[0:16:1], [0:2:1], [0:4:1], [0:512:2]} | slice | bytes 131072 | tf_op jit(solution)/shard_map/slice | solution.py:42
  216.3 3.2 %slice.777 = bf16[16,2,4,256]{3,0,2,1:T(8,128)(2,1)S(1)} slice(bf16[16,2,4,512]{3,0,2,1:T(8,128)(2,1)} %pad_maximum_fusion.35), slice={[0:16:1], [0:2:1], [0:4:1], [0:512:2]} | slice | bytes 131072 | tf_op jit(solution)/shard_map/slice | solution.py:42
  254.5 9.5 %psum.30 = f32[27,32,16]{1,2,0:T(8,128)S(1)} all-reduce(f32[27,32,16]{1,2,0:T(8,128)S(1)} %fusion.16), channel_id=1, replica_groups=mesh['groups'=2,'gz'=4,'sec'=2,'ch'=2] {'sec'}, use_global_device_ids=true, to_apply=%region_3.4 | all-reduce | flops 13824 | bytes 110592 | tf_op jit(solution)/shard_map/psum | solution.py:99
  264.0 22.0 %psum.31 = f32[27,32,16]{1,2,0:T(8,128)S(1)} all-reduce(f32[27,32,16]{1,2,0:T(8,128)S(1)} %psum.30), channel_id=1, replica_groups=mesh['groups'=2,'gz'=4,'sec'=2,'ch'=2] {'gz'}, use_global_device_ids=true, to_apply=%region_4.5 | all-reduce | flops 13824 | bytes 110592 | tf_op jit(solution)/shard_map/psum | solution.py:98
  288.3 5.5 %reduce-scatter.2.cloned.1.call-done = f32[32,2,4,256]{3,0,2,1:T(8,128)} async-done(((f32[64,2,4,256]{3,0,2,1:T(8,128)}), f32[32,2,4,256]{3,0,2,1:T(8,128)}) %reduce-scatter.2.cloned.1.call-update) | async-done | bytes 262160 | tf_op jit(solution)/shard_map/reduce_scatter | solution.py:96
  (249 shorter events, 159.1 us)
Async XLA Ops:
  7.2 80.6 %copy-start = (bf16[27,32,32]{2,1,0:T(8,128)(2,1)S(1)}, bf16[27,32,32]{2,1,0:T(8,128)(2,1)}, u32[]{:S(2)}) copy-start(bf16[27,32,32]{2,1,0:T(8,128)(2,1)} %param.9) | copy-start | bytes 165892
  7.2 14.1 %all-gather.2.cloned.1.call-start = ((), (), s32[]{:S(2)}) async-start(), calls=%async_computation.1 | async-start | bytes 1572864 | tf_op jit(solution)/shard_map/all_gather | solution.py:56
  9.4 240.5 %all-reduce.5.cloned.1.call-start = ((), (), s32[]{:S(2)}) async-start(), calls=%async_computation.3 | async-start | bytes 442368 | tf_op jit(solution)/shard_map/psum | solution.py:99
  21.3 6.1 %copy-start.1 = (bf16[32,4,8,512]{3,0,2,1:T(8,128)(2,1)S(1)}, bf16[32,4,8,512]{3,0,2,1:T(8,128)(2,1)}, u32[]{:S(2)}) copy-start(bf16[32,4,8,512]{3,0,2,1:T(8,128)(2,1)} %all-gather.2.cloned.1.call-done) | copy-start | bytes 3145732
  22.7 24.7 %collective-permute-start = (bf16[32,2,8,512]{3,0,2,1:T(8,128)(2,1)S(1)}, bf16[32,2,8,512]{3,0,2,1:T(8,128)(2,1)S(1)}, u32[]{:S(2)}, u32[]{:S(2)}) collective-permute-start(bf16[32,2,8,512]{3,0,2,1:T(8,128)(2,1)S(1)} %get-tuple-element.50), channel_id=1, source_target_pairs={{0,2},{2,4},{4,6},{6,8},{8,10},{10,12},{12,14},{14,0},{1,3},{3,5},... | collective-permute-start | bytes 1572872 | tf_op jit(solution)/shard_map/ppermute | solution.py:15
  24.5 25.1 %collective-permute-start.1 = (bf16[32,2,8,512]{3,0,2,1:T(8,128)(2,1)S(1)}, bf16[32,2,8,512]{3,0,2,1:T(8,128)(2,1)S(1)}, u32[]{:S(2)}, u32[]{:S(2)}) collective-permute-start(bf16[32,2,8,512]{3,0,2,1:T(8,128)(2,1)S(1)} %get-tuple-element.51), channel_id=1, source_target_pairs={{2,0},{4,2},{6,4},{8,6},{10,8},{12,10},{14,12},{0,14},{3,1},{5,3},... | collective-permute-start | bytes 1572872 | tf_op jit(solution)/shard_map/ppermute | solution.py:18
  59.9 1.0 copy-start.11
  60.9 1.0 copy-start.14
  66.9 1.0 copy-start.9
  70.4 1.0 copy-start.7
  77.0 1.0 copy-start.5
  101.3 7.7 %collective-permute-start.2 = (bf16[16,1,8,512]{3,0,2,1:T(8,128)(2,1)S(1)}, bf16[16,1,8,512]{3,0,2,1:T(8,128)(2,1)S(1)}, u32[]{:S(2)}, u32[]{:S(2)}) collective-permute-start(bf16[16,1,8,512]{3,0,2,1:T(8,128)(2,1)S(1)} %slice.824), channel_id=1, source_target_pairs={{14,0},{0,2},{2,4},{4,6},{6,8},{8,10},{10,12},{12,14},{15,1},{1,3}... | collective-permute-start | bytes 393224 | tf_op jit(solution)/shard_map/ppermute | solution.py:26
  102.5 7.5 %copy-start.17 = (f32[27,32,16]{1,2,0:T(8,128)}, f32[27,32,16]{1,2,0:T(8,128)S(1)}, u32[]{:S(2)}) copy-start(f32[27,32,16]{1,2,0:T(8,128)S(1)} %fusion.18) | copy-start | bytes 165892
  127.8 23.9 %copy-start.23 = (bf16[16,2,4,1]{3,0,2,1:T(8,128)(2,1)S(1)}, bf16[16,2,4,1]{3,0,2,1:T(8,128)(2,1)}, u32[]{:S(2)}) copy-start(bf16[16,2,4,1]{3,0,2,1:T(8,128)(2,1)} %get-tuple-element.91) | copy-start | bytes 772
  128.6 26.7 %copy-start.24 = (bf16[16,2,4,1]{3,0,2,1:T(8,128)(2,1)S(1)}, bf16[16,2,4,1]{3,0,2,1:T(8,128)(2,1)}, u32[]{:S(2)}) copy-start(bf16[16,2,4,1]{3,0,2,1:T(8,128)(2,1)} %get-tuple-element.88) | copy-start | bytes 772
  131.7 28.4 %copy-start.21 = (bf16[16,2,4,1]{3,0,2,1:T(8,128)(2,1)S(1)}, bf16[16,2,4,1]{3,0,2,1:T(8,128)(2,1)}, u32[]{:S(2)}) copy-start(bf16[16,2,4,1]{3,0,2,1:T(8,128)(2,1)} %get-tuple-element.87) | copy-start | bytes 772
  134.7 30.2 %copy-start.22 = (bf16[16,2,4,1]{3,0,2,1:T(8,128)(2,1)S(1)}, bf16[16,2,4,1]{3,0,2,1:T(8,128)(2,1)}, u32[]{:S(2)}) copy-start(bf16[16,2,4,1]{3,0,2,1:T(8,128)(2,1)} %get-tuple-element.84) | copy-start | bytes 772
  148.3 43.8 %copy-start.20 = (bf16[16,2,4,1]{3,0,2,1:T(8,128)(2,1)S(1)}, bf16[16,2,4,1]{3,0,2,1:T(8,128)(2,1)}, u32[]{:S(2)}) copy-start(bf16[16,2,4,1]{3,0,2,1:T(8,128)(2,1)} %get-tuple-element.72) | copy-start | bytes 772
  155.3 46.5 %copy-start.19 = (bf16[16,2,4,1]{3,0,2,1:T(8,128)(2,1)S(1)}, bf16[16,2,4,1]{3,0,2,1:T(8,128)(2,1)}, u32[]{:S(2)}) copy-start(bf16[16,2,4,1]{3,0,2,1:T(8,128)(2,1)} %get-tuple-element.68) | copy-start | bytes 772
  225.2 61.5 %all-reduce.7.cloned.1.call-start = ((), (), s32[]{:S(2)}) async-start(), calls=%async_computation.4 | async-start | bytes 442368 | tf_op jit(solution)/shard_map/psum | solution.py:98
  247.9 3.9 %copy-start.2 = (bf16[32,4,8,512]{3,0,2,1:T(8,128)(2,1)S(1)}, bf16[32,4,8,512]{3,0,2,1:T(8,128)(2,1)}, u32[]{:S(2)}) copy-start(bf16[32,4,8,512]{3,0,2,1:T(8,128)(2,1)} %get-tuple-element.6) | copy-start | bytes 3145732
  247.9 3.9 %copy-start.18 = (f32[27,32,16]{1,2,0:T(8,128)S(1)}, f32[27,32,16]{1,2,0:T(8,128)}, u32[]{:S(2)}) copy-start(f32[27,32,16]{1,2,0:T(8,128)} %copy-done.17) | copy-start | bytes 165892
  250.0 43.9 %reduce-scatter.2.cloned.1.call-start = ((), (), s32[]{:S(2)}) async-start(), calls=%async_computation.2 | async-start | bytes 786432 | tf_op jit(solution)/shard_map/reduce_scatter | solution.py:96
  251.8 1.9 copy-start.15
  (8 other events, 7.4 us)
Sparse Core Ops, SparseCore 0:
  9.6 11.7 all-gather.1
  225.3 20.9 all-reduce.4
  250.1 34.1 all-reduce.6
  286.5 7.3 reduce-scatter.1
